TPU v7x, 128 devices: a whole 4x4x4 slice. The times are simulated.
128 devices in a mesh: seq: 32 (over y, z, core), head: 4 (over x).
Axes of the slice: x: 4, y: 4, z: 4, core: 2. Of those that a mesh axis runs over, the one named last changes fastest.
Arguments:
- queries: bfloat16 [8192, 2048], P('seq', 'head'), parts along dimension 1, may hold values from -6 to 6
- keys: bfloat16 [8192, 512], P('seq', 'head'), parts along dimension 1, may hold values from -6 to 6
- values: bfloat16 [8192, 512], P('seq', 'head'), parts along dimension 1, may hold values from -6 to 6
- grad_out: bfloat16 [8192, 2048], P('seq', 'head'), parts along dimension 1, may hold values from -6 to 6
- lengths: int32 [16], replicated, may hold values from 1 to 2048, 8192 in all
- send_order: int32 [32, 256], replicated, may hold values from 0 to 255, each once within a row
Outputs:
- attended: float32 [8192, 2048], P('seq', 'head'), parts along dimension 1
- grad_queries: float32 [8192, 2048], P('seq', 'head'), parts along dimension 1
- grad_keys: float32 [8192, 512], P('seq', 'head'), parts along dimension 1
- grad_values: float32 [8192, 512], P('seq', 'head'), parts along dimension 1
There are 4 independent parts, one for each index of `head`. A program takes and returns all parts, laid end to end along the dimension named above; an argument that names none is the same for every part. Nothing has to cross between parts.
Inputs may be any that keep to these rules, and one draw needn't show every extreme that they name: `lengths`: they sum to 8192; the longest is exactly 2048. `send_order`: each row is a permutation of 0 to 255.
All inputs are finite; a program needn't handle non-finite values.
Results may differ from a plain program's by a relative error of at most 0.039.
Values may be sent and summed in bfloat16 or wider, within the bound.
No kernel may reach another device: no remote copies, remote signals or barrier semaphores. Data moves between devices by JAX's collectives and lax.ppermute only.
A program may use at most 64 MiB of HBM per device.

v0:
```python
import math
import jax
import jax.numpy as jnp
from jax import lax
from jax.sharding import PartitionSpec as P

masked_value = -1e30


def doc_index(positions, bounds):
    return jnp.sum((positions[:, None] >= bounds[None, :]).astype(jnp.int32), axis=1)


def visible(query_pos, query_doc, key_pos, bounds):
    key_doc = doc_index(key_pos, bounds)
    return ((query_doc[:, None] == key_doc[None, :]) & (key_pos[None, :] <= query_pos[:, None]))[
        :, None, :
    ]


def block_scores(query_heads, key_block, allowed, score_scale):
    products = (
        jnp.einsum("bhd,td->bht", query_heads, key_block, preferred_element_type=jnp.float32)
        * score_scale
    )
    return jnp.where(allowed, products, masked_value)


def key_blocks(key_piece, value_piece):
    piece_rows = key_piece.shape[0]
    block_rows = math.gcd(piece_rows, 512)
    block_count = piece_rows // block_rows
    offsets = block_rows * jnp.arange(block_count, dtype=jnp.int32)
    stacked = (
        key_piece.reshape(block_count, block_rows, key_piece.shape[1]),
        value_piece.reshape(block_count, block_rows, value_piece.shape[1]),
        offsets,
    )
    return (stacked, block_rows)


def forward_piece(run_state, key_piece, value_piece, context):
    query_heads, query_pos, query_doc, bounds, score_scale = context
    stacked, block_rows = key_blocks(key_piece, value_piece)

    def forward_update(loop_state, block_item):
        run_max, run_total, weighted = loop_state
        key_block, value_block, offset = block_item
        allowed = visible(
            query_pos, query_doc, offset + jnp.arange(block_rows, dtype=jnp.int32), bounds
        )
        scores = block_scores(query_heads, key_block, allowed, score_scale)
        new_max = jnp.maximum(run_max, jnp.max(scores, axis=2))
        exp_weights = jnp.where(allowed, jnp.exp(scores - new_max[:, :, None]), 0.0)
        rescale = jnp.exp(run_max - new_max)
        run_total = run_total * rescale + jnp.sum(exp_weights, axis=2)
        weighted = weighted * rescale[:, :, None] + jnp.einsum(
            "bht,td->bhd",
            exp_weights.astype(jnp.bfloat16),
            value_block,
            preferred_element_type=jnp.float32,
        )
        return ((new_max, run_total, weighted), None)

    run_state, _ = lax.scan(forward_update, run_state, stacked)
    return run_state


def backward_piece(key_piece, value_piece, context):
    query_heads, grad_heads, query_pos, query_doc, bounds, score_scale, log_total, out_dot = context
    stacked, block_rows = key_blocks(key_piece, value_piece)

    def backward_update(query_sum, block_item):
        key_block, value_block, offset = block_item
        allowed = visible(
            query_pos, query_doc, offset + jnp.arange(block_rows, dtype=jnp.int32), bounds
        )
        scores = block_scores(query_heads, key_block, allowed, score_scale)
        weights = jnp.where(allowed, jnp.exp(scores - log_total[:, :, None]), 0.0)
        grad_dots = jnp.einsum(
            "bhd,td->bht", grad_heads, value_block, preferred_element_type=jnp.float32
        )
        score_grads = (weights * (grad_dots - out_dot[:, :, None])).astype(jnp.bfloat16)
        query_sum = query_sum + jnp.einsum(
            "bht,td->bhd", score_grads, key_block, preferred_element_type=jnp.float32
        )
        key_term = (
            jnp.einsum("bht,bhd->td", score_grads, query_heads, preferred_element_type=jnp.float32)
            * score_scale
        )
        value_term = jnp.einsum(
            "bht,bhd->td",
            weights.astype(jnp.bfloat16),
            grad_heads,
            preferred_element_type=jnp.float32,
        )
        return (query_sum, (key_term, value_term))

    zero_query = jnp.zeros(query_heads.shape, jnp.float32)
    query_add, (key_terms, value_terms) = lax.scan(backward_update, zero_query, stacked)
    piece_rows = key_piece.shape[0]
    return (query_add, key_terms.reshape(piece_rows, -1), value_terms.reshape(piece_rows, -1))


def per_device(queries, keys, values, grad_out, lengths, send_order):
    shard_count = lax.axis_size("seq")
    my_index = lax.axis_index("seq")
    tok_rows, head_dim = keys.shape
    group_rows = tok_rows // shard_count
    head_count = queries.shape[1] // head_dim
    score_scale = 1.0 / math.sqrt(head_dim)
    bounds = jnp.cumsum(lengths)
    own_order = lax.dynamic_index_in_dim(send_order, my_index, 0, keepdims=False)
    outgoing = jnp.take(queries, own_order, axis=0)
    picked = lax.all_to_all(outgoing, "seq", split_axis=0, concat_axis=0, tiled=True)
    columns = lax.dynamic_slice_in_dim(send_order, my_index * group_rows, group_rows, 1)
    query_pos = (jnp.arange(shard_count, dtype=jnp.int32)[:, None] * tok_rows + columns).reshape(
        tok_rows
    )
    query_doc = doc_index(query_pos, bounds)
    query_heads = picked.reshape(tok_rows, head_count, head_dim)
    grad_heads = grad_out.reshape(tok_rows, head_count, head_dim)
    context = (query_heads, query_pos, query_doc, bounds, score_scale)
    start_state = (
        jnp.full((tok_rows, head_count), masked_value, jnp.float32),
        jnp.zeros((tok_rows, head_count), jnp.float32),
        jnp.zeros((tok_rows, head_count, head_dim), jnp.float32),
    )
    piece_pair = (
        lax.all_gather(keys, "seq", axis=0, tiled=True),
        lax.all_gather(values, "seq", axis=0, tiled=True),
    )
    run_max, run_total, weighted = forward_piece(start_state, piece_pair[0], piece_pair[1], context)
    attended = weighted / run_total[:, :, None]
    attended_low = attended.astype(jnp.bfloat16)
    log_total = run_max + jnp.log(run_total)
    out_dot = jnp.sum(grad_heads.astype(jnp.float32) * attended_low.astype(jnp.float32), axis=2)
    grad_context = (
        query_heads,
        grad_heads,
        query_pos,
        query_doc,
        bounds,
        score_scale,
        log_total,
        out_dot,
    )
    piece_pair = (
        lax.all_gather(keys, "seq", axis=0, tiled=True),
        lax.all_gather(values, "seq", axis=0, tiled=True),
    )
    query_add, key_part, value_part = backward_piece(piece_pair[0], piece_pair[1], grad_context)
    key_all = key_part
    value_all = value_part
    query_sum, key_all, value_all = (query_add, key_all, value_all)
    key_grad, value_grad = (
        lax.psum_scatter(key_all, "seq", scatter_dimension=0, tiled=True),
        lax.psum_scatter(value_all, "seq", scatter_dimension=0, tiled=True),
    )
    grad_queries = (query_sum * score_scale).reshape(tok_rows, head_count * head_dim)
    return (attended.reshape(tok_rows, head_count * head_dim), grad_queries, key_grad, value_grad)


def solution(mesh):
    placed = (P("seq", "head"), P("seq", "head"), P("seq", "head"), P("seq", "head"), P(), P())
    return jax.shard_map(
        per_device,
        mesh=mesh,
        in_specs=placed,
        out_specs=(P("seq", "head"), P("seq", "head"), P("seq", "head"), P("seq", "head")),
        check_vma=False,
    )
```

profile of v0, /device:TPU:0, one launch (start us, length us, event | category | flops | bytes accessed | tf_op | source)
XLA Modules:
  0.0 495.6 jit_solution(17738057707198617605)
XLA Ops:
  12.2 8.4 %all-to-all-start = ((bf16[32,8,512]{2,1,0:T(8,128)(2,1)}), bf16[32,8,512]{2,1,0:T(8,128)(2,1)S(1)}, u32[]{:S(2)}, u32[]{:S(2)}) async-start(bf16[32,8,512]{2,1,0:T(8,128)(2,1)} %bitcast_select_fusion.2), calls=%async_computation | async-start | bytes 524288 | tf_op jit(solution)/shard_map/all_to_all | solution.py:115
  21.8 8.0 %all-to-all-done = bf16[32,8,512]{2,1,0:T(8,128)(2,1)S(1)} async-done(((bf16[32,8,512]{2,1,0:T(8,128)(2,1)}), bf16[32,8,512]{2,1,0:T(8,128)(2,1)S(1)}, u32[]{:S(2)}, u32[]{:S(2)}) %all-to-all-start) | async-done | bytes 262176 | tf_op jit(solution)/shard_map/all_to_all | solution.py:115
  29.9 26.8 %all-gather.3.cloned.1.call-done = bf16[8192,128]{1,0:T(8,128)(2,1)} async-done(((bf16[256,128]{1,0:T(8,128)(2,1)}), bf16[8192,128]{1,0:T(8,128)(2,1)}) %all-gather.3.cloned.1.call-update) | async-done | bytes 2097168 | tf_op jit(solution)/shard_map/all_gather | solution.py:130
  56.7 45.3 %all-gather.5.cloned.1.call-done = bf16[8192,128]{1,0:T(8,128)(2,1)} async-done(((bf16[256,128]{1,0:T(8,128)(2,1)}), bf16[8192,128]{1,0:T(8,128)(2,1)}) %all-gather.5.cloned.1.call-update) | async-done | bytes 2097168 | tf_op jit(solution)/shard_map/all_gather | solution.py:131
  102.0 85.3 %while.32 = (s32[]{:T(128)}, f32[256,4]{0,1:T(4,128)S(1)}, f32[256,4]{0,1:T(4,128)S(1)}, f32[256,4,128]{2,0,1:T(8,128)S(1)}, s32[256]{0:T(256)S(1)}, /*index=5*/...) while((s32[]{:T(128)}, f32[256,4]{0,1:T(4,128)S(1)}, ...), condition=%wide.wide.region_6.7_spmd.clone, body=%wide.wide.region_2.6_spmd.clone.sunk | while | flops 276067328 | bytes 8466673 | solution.py:65
  105.5 1.8 convolution_add_fusion.6
  110.8 1.8 convolution_add_fusion.6
  116.2 1.8 convolution_add_fusion.6
  121.5 1.8 convolution_add_fusion.6
  126.8 1.8 convolution_add_fusion.6
  132.1 1.8 convolution_add_fusion.6
  137.5 1.8 convolution_add_fusion.6
  142.8 1.8 convolution_add_fusion.6
  148.1 1.8 convolution_add_fusion.6
  153.5 1.8 convolution_add_fusion.6
  158.8 1.8 convolution_add_fusion.6
  164.1 1.8 convolution_add_fusion.6
  169.5 1.8 convolution_add_fusion.6
  174.8 1.8 convolution_add_fusion.6
  180.1 1.8 convolution_add_fusion.6
  185.5 1.8 convolution_add_fusion.6
  187.6 133.8 %while.33 = (s32[]{:T(128)}, f32[256,4,128]{2,0,1:T(8,128)S(1)}, f32[16,512,128]{2,1,0:T(8,128)}, f32[16,512,128]{2,1,0:T(8,128)}, s32[256]{0:T(256)S(1)}, /*ind...) while((s32[]{:T(128)}, f32[256,4,128]{2,0,1:T(8,128)S(1)}, ...), condition=%wide.wide.region_10.11_spmd.clone, body=%wide.wide.region_8.10_spmd.clone.sunk | while | flops 676028416 | bytes 12734739 | solution.py:100
  323.9 79.4 %reduce-scatter.5.cloned.1.call-done = f32[256,128]{1,0:T(8,128)} async-done(((f32[8192,128]{1,0:T(8,128)}), f32[256,128]{1,0:T(8,128)}) %reduce-scatter.5.cloned.1.call-update) | async-done | bytes 131088 | tf_op jit(solution)/shard_map/reduce_scatter | solution.py:158
  403.3 85.8 %reduce-scatter.3.cloned.1.call-done = f32[256,128]{1,0:T(8,128)} async-done(((f32[8192,128]{1,0:T(8,128)}), f32[256,128]{1,0:T(8,128)}) %reduce-scatter.3.cloned.1.call-update) | async-done | bytes 131088 | tf_op jit(solution)/shard_map/reduce_scatter | solution.py:157
  (338 shorter events, 197.6 us)
Async XLA Ops:
  7.2 3.1 copy-start
  7.2 13.5 %copy-start.3 = (s32[32,256]{1,0:T(8,128)S(1)}, s32[32,256]{1,0:T(8,128)}, u32[]{:S(2)}) copy-start(s32[32,256]{1,0:T(8,128)} %param.15) | copy-start | bytes 98308
  7.2 13.9 %copy-start.4 = (s32[16]{0:T(128)S(1)}, s32[16]{0:T(128)}, u32[]{:S(2)}) copy-start(s32[16]{0:T(128)} %param.14) | copy-start | bytes 196
  7.2 14.2 %copy-start.1 = (bf16[256,512]{1,0:T(8,128)(2,1)S(1)}, bf16[256,512]{1,0:T(8,128)(2,1)}, u32[]{:S(2)}) copy-start(bf16[256,512]{1,0:T(8,128)(2,1)} %param.13) | copy-start | bytes 786436
  7.2 49.5 %all-gather.3.cloned.1.call-start = ((), (), s32[]{:S(2)}) async-start(), calls=%async_computation.3 | async-start | bytes 2162688 | tf_op jit(solution)/shard_map/all_gather | solution.py:130
  7.9 94.0 %all-gather.5.cloned.1.call-start = ((), (), s32[]{:S(2)}) async-start(), calls=%async_computation.4 | async-start | bytes 2162688 | tf_op jit(solution)/shard_map/all_gather | solution.py:131
  12.2 17.5 %all-to-all-start = ((bf16[32,8,512]{2,1,0:T(8,128)(2,1)}), bf16[32,8,512]{2,1,0:T(8,128)(2,1)S(1)}, u32[]{:S(2)}, u32[]{:S(2)}) async-start(bf16[32,8,512]{2,1,0:T(8,128)(2,1)} %bitcast_select_fusion.2), calls=%async_computation | async-start | bytes 524288 | tf_op jit(solution)/shard_map/all_to_all | solution.py:115
  20.7 382.6 %reduce-scatter.5.cloned.1.call-start = ((), (), s32[]{:S(2)}) async-start(), calls=%async_computation.6 | async-start | bytes 4325376 | tf_op jit(solution)/shard_map/reduce_scatter | solution.py:158
  20.8 81.2 %copy-start.2 = (s32[32,8]{1,0:T(8,128)}, s32[32,8]{1,0:T(8,128)S(1)}, u32[]{:S(2)}) copy-start(s32[32,8]{1,0:T(8,128)S(1)} %dynamic-slice_add_fusion) | copy-start | bytes 3076
  321.4 167.7 %reduce-scatter.3.cloned.1.call-start = ((), (), s32[]{:S(2)}) async-start(), calls=%async_computation.5 | async-start | bytes 4325376 | tf_op jit(solution)/shard_map/reduce_scatter | solution.py:157
Sparse Core Ops, SparseCore 0:
  10.3 46.3 all-gather.2
  59.0 42.9 all-gather.4
  321.5 81.6 reduce-scatter.4
  407.3 81.6 reduce-scatter.2
where the time goes:
time: 498 us; the launch traced here: 496 us
  waiting for transfers between devices  247 us (50%)
  matrix products  160 us (32%)
  other arithmetic  41.9 us (8%)
  local copies, waits for them, and re-layouts  22.7 us (5%)
  between operations  14 us (3%)
  starting transfers between devices  8.6 us (2%)
    reduce_scatter x1, waiting for transfers between devices, per_device(): lax.psum_scatter(key_all, 'seq', scatter_dimension=0, tiled=True)  85.8 us
    reduce_scatter x1, waiting for transfers between devices, per_device(): lax.psum_scatter(value_all, 'seq', scatter_dimension=0, tiled=True)  79.4 us
    dot_general x32, matrix products, block_scores(): jnp.einsum('bhd,td->bht', query_heads, key_block, preferred_element_type=...  47.9 us
    all_gather x1, waiting for transfers between devices, per_device(): lax.all_gather(values, 'seq', axis=0, tiled=True)  45.3 us
    dot_general x16, matrix products, forward_update(): jnp.einsum('bht,td->bhd', exp_weights.astype(jnp.bfloat16), value_block,...  28.7 us
    all_gather x1, waiting for transfers between devices, per_device(): lax.all_gather(keys, 'seq', axis=0, tiled=True)  26.8 us
    dot_general x16, matrix products, backward_update(): jnp.einsum('bht,td->bhd', score_grads, key_block, preferred_element_type=...  24.8 us
    dot_general x16, matrix products, backward_update(): jnp.einsum('bhd,td->bht', grad_heads, value_block, preferred_element_type...  21.5 us
  transfers between devices with their start and end apart: 5, of which 5 were waited for; matrix products, arithmetic and copies ran while one was open for 1% of the time, Pallas kernels for 0%

commit v1 on v0

--- a/solution.py
+++ b/solution.py
@@ -5,6 +5,11 @@
 from jax.sharding import PartitionSpec as P
 
 masked_value = -1e30
+
+
+def gather_by_exchange(x, axis, dim):
+    copies = jnp.concatenate([x] * lax.axis_size(axis), axis=dim)
+    return lax.all_to_all(copies, axis, dim, dim, tiled=True)
 
 
 def doc_index(positions, bounds):
@@ -128,7 +133,7 @@
     )
     piece_pair = (
         lax.all_gather(keys, "seq", axis=0, tiled=True),
-        lax.all_gather(values, "seq", axis=0, tiled=True),
+        gather_by_exchange(values, "seq", 0),
     )
     run_max, run_total, weighted = forward_piece(start_state, piece_pair[0], piece_pair[1], context)
     attended = weighted / run_total[:, :, None]

time: 498 us -> 472 us (0.948)
  waiting for transfers between devices: 247 us -> 194 us
  local copies, waits for them, and re-layouts: 22.7 us -> 42.6 us
  starting transfers between devices: 8.6 us -> 16.3 us
    all_gather x1, waiting for transfers between devices: 45.3 us -> 0.02 us  [per_device(): lax.all_gather(values, 'seq', axis=0, tiled=True)]
    all_to_all x0 -> x1, waiting for transfers between devices: none -> 28 us  [gather_by_exchange(): return lax.all_to_all(copies, axis, dim, dim, tiled=True)]
    all_gather x1, waiting for transfers between devices: 26.8 us -> 0.01 us  [per_device(): lax.all_gather(keys, 'seq', axis=0, tiled=True)]
    unnamed x14 -> x47, local copies, waits for them, and re-layouts: 1.36 us -> 20.7 us
    all_to_all x1, waiting for transfers between devices: 7.96 us -> 0.01 us  [per_device(): lax.all_to_all(outgoing, 'seq', split_axis=0, concat_axis=0, tiled=True)]
    all_to_all x0 -> x1, starting transfers between devices: none -> 7.65 us  [gather_by_exchange(): return lax.all_to_all(copies, axis, dim, dim, tiled=True)]
  transfers between devices with their start and end apart: 5 -> 6, of which waited for: 5 -> 3; matrix products, arithmetic and copies ran while one was open for 1% -> 24% of each run, Pallas kernels for 0% -> 0%
where the time goes in v1:
time: 472 us; the launch traced here: 470 us
  waiting for transfers between devices  194 us (41%)
  matrix products  160 us (34%)
  local copies, waits for them, and re-layouts  42.6 us (9%)
  other arithmetic  41.9 us (9%)
  starting transfers between devices  16.3 us (3%)
  between operations  14 us (3%)
    reduce_scatter x1, waiting for transfers between devices, per_device(): lax.psum_scatter(key_all, 'seq', scatter_dimension=0, tiled=True)  85.9 us
    reduce_scatter x1, waiting for transfers between devices, per_device(): lax.psum_scatter(value_all, 'seq', scatter_dimension=0, tiled=True)  77.9 us
    dot_general x32, matrix products, block_scores(): jnp.einsum('bhd,td->bht', query_heads, key_block, preferred_element_type=...  47.9 us
    dot_general x16, matrix products, forward_update(): jnp.einsum('bht,td->bhd', exp_weights.astype(jnp.bfloat16), value_block,...  28.7 us
    all_to_all x1, waiting for transfers between devices, gather_by_exchange(): return lax.all_to_all(copies, axis, dim, dim, tiled=True)  28 us
    dot_general x16, matrix products, backward_update(): jnp.einsum('bht,td->bhd', score_grads, key_block, preferred_element_type=...  24.9 us
    dot_general x16, matrix products, backward_update(): jnp.einsum('bhd,td->bht', grad_heads, value_block, preferred_element_type...  21.5 us
    unnamed x47, local copies, waits for them, and re-layouts  20.7 us
  transfers between devices with their start and end apart: 6, of which 3 were waited for; matrix products, arithmetic and copies ran while one was open for 24% of the time, Pallas kernels for 0%

profile of v1, /device:TPU:0, one launch (start us, length us, event | category | flops | bytes accessed | tf_op | source)
XLA Modules:
  0.0 469.8 jit_solution(7992012147603851528)
XLA Ops:
  11.4 8.4 %all-to-all-start = ((bf16[32,8,512]{2,1,0:T(8,128)(2,1)}), bf16[32,8,512]{2,1,0:T(8,128)(2,1)S(1)}, u32[]{:S(2)}, u32[]{:S(2)}) async-start(bf16[32,8,512]{2,1,0:T(8,128)(2,1)} %bitcast_select_fusion.2), calls=%async_computation | async-start | bytes 524288 | tf_op jit(solution)/shard_map/all_to_all | solution.py:120
  39.8 7.7 %all-to-all-start.1 = ((bf16[32,256,128]{2,1,0:T(8,128)(2,1)}), bf16[32,256,128]{2,1,0:T(8,128)(2,1)}, u32[]{:S(2)}, u32[]{:S(2)}) async-start(bf16[32,256,128]{2,1,0:T(8,128)(2,1)} %bitcast.5), calls=%async_computation.1 | async-start | bytes 4194304 | tf_op jit(solution)/shard_map/all_to_all | solution.py:12
  49.5 28.0 %all-to-all-done.1 = bf16[32,256,128]{2,1,0:T(8,128)(2,1)} async-done(((bf16[32,256,128]{2,1,0:T(8,128)(2,1)}), bf16[32,256,128]{2,1,0:T(8,128)(2,1)}, u32[]{:S(2)}, u32[]{:S(2)}) %all-to-all-start.1) | async-done | bytes 2097184 | tf_op jit(solution)/shard_map/all_to_all | solution.py:12
  77.6 85.3 %while.32 = (s32[]{:T(128)}, f32[256,4]{0,1:T(4,128)S(1)}, f32[256,4]{0,1:T(4,128)S(1)}, f32[256,4,128]{2,0,1:T(8,128)S(1)}, s32[256]{0:T(256)S(1)}, /*index=5*/...) while((s32[]{:T(128)}, f32[256,4]{0,1:T(4,128)S(1)}, ...), condition=%wide.wide.region_6.7_spmd.clone, body=%wide.wide.region_2.6_spmd.clone.sunk | while | flops 276067328 | bytes 8466673 | solution.py:70
  81.1 1.8 convolution_add_fusion.6
  86.4 1.8 convolution_add_fusion.6
  91.7 1.8 convolution_add_fusion.6
  97.1 1.8 convolution_add_fusion.6
  102.4 1.8 convolution_add_fusion.6
  107.7 1.8 convolution_add_fusion.6
  113.1 1.8 convolution_add_fusion.6
  118.4 1.8 convolution_add_fusion.6
  123.7 1.8 convolution_add_fusion.6
  129.0 1.8 convolution_add_fusion.6
  134.4 1.8 convolution_add_fusion.6
  139.7 1.8 convolution_add_fusion.6
  145.0 1.8 convolution_add_fusion.6
  150.4 1.8 convolution_add_fusion.6
  155.7 1.8 convolution_add_fusion.6
  161.0 1.8 convolution_add_fusion.6
  163.2 133.8 %while.33 = (s32[]{:T(128)}, f32[256,4,128]{2,0,1:T(8,128)S(1)}, f32[16,512,128]{2,1,0:T(8,128)}, f32[16,512,128]{2,1,0:T(8,128)}, s32[256]{0:T(256)S(1)}, /*ind...) while((s32[]{:T(128)}, f32[256,4,128]{2,0,1:T(8,128)S(1)}, ...), condition=%wide.wide.region_10.11_spmd.clone, body=%wide.wide.region_8.10_spmd.clone.sunk | while | flops 676028416 | bytes 12734739 | solution.py:105
  181.4 1.6 fusion.101
  299.5 77.9 %reduce-scatter.5.cloned.1.call-done = f32[256,128]{1,0:T(8,128)} async-done(((f32[8192,128]{1,0:T(8,128)}), f32[256,128]{1,0:T(8,128)}) %reduce-scatter.5.cloned.1.call-update) | async-done | bytes 131088 | tf_op jit(solution)/shard_map/reduce_scatter | solution.py:163
  377.3 85.9 %reduce-scatter.3.cloned.1.call-done = f32[256,128]{1,0:T(8,128)} async-done(((f32[8192,128]{1,0:T(8,128)}), f32[256,128]{1,0:T(8,128)}) %reduce-scatter.3.cloned.1.call-update) | async-done | bytes 131088 | tf_op jit(solution)/shard_map/reduce_scatter | solution.py:162
  (374 shorter events, 216.0 us)
Async XLA Ops:
  7.2 2.3 copy-start
  7.2 12.7 %copy-start.1 = (bf16[256,128]{1,0:T(8,128)(2,1)S(1)}, bf16[256,128]{1,0:T(8,128)(2,1)}, u32[]{:S(2)}) copy-start(bf16[256,128]{1,0:T(8,128)(2,1)} %param.12) | copy-start | bytes 196612
  7.2 70.4 %all-gather.3.cloned.1.call-start = ((), (), s32[]{:S(2)}) async-start(), calls=%async_computation.4 | async-start | bytes 2162688 | tf_op jit(solution)/shard_map/all_gather | solution.py:135
  11.4 28.4 %all-to-all-start = ((bf16[32,8,512]{2,1,0:T(8,128)(2,1)}), bf16[32,8,512]{2,1,0:T(8,128)(2,1)S(1)}, u32[]{:S(2)}, u32[]{:S(2)}) async-start(bf16[32,8,512]{2,1,0:T(8,128)(2,1)} %bitcast_select_fusion.2), calls=%async_computation | async-start | bytes 524288 | tf_op jit(solution)/shard_map/all_to_all | solution.py:120
  39.8 8.5 %copy-start.4 = (s32[32,256]{1,0:T(8,128)S(1)}, s32[32,256]{1,0:T(8,128)}, u32[]{:S(2)}) copy-start(s32[32,256]{1,0:T(8,128)} %param.15) | copy-start | bytes 98308
  39.8 8.9 %copy-start.5 = (s32[16]{0:T(128)S(1)}, s32[16]{0:T(128)}, u32[]{:S(2)}) copy-start(s32[16]{0:T(128)} %param.14) | copy-start | bytes 196
  39.8 9.2 %copy-start.2 = (bf16[256,512]{1,0:T(8,128)(2,1)S(1)}, bf16[256,512]{1,0:T(8,128)(2,1)}, u32[]{:S(2)}) copy-start(bf16[256,512]{1,0:T(8,128)(2,1)} %param.13) | copy-start | bytes 786436
  39.8 37.7 %all-to-all-start.1 = ((bf16[32,256,128]{2,1,0:T(8,128)(2,1)}), bf16[32,256,128]{2,1,0:T(8,128)(2,1)}, u32[]{:S(2)}, u32[]{:S(2)}) async-start(bf16[32,256,128]{2,1,0:T(8,128)(2,1)} %bitcast.5), calls=%async_computation.1 | async-start | bytes 4194304 | tf_op jit(solution)/shard_map/all_to_all | solution.py:12
  47.5 115.7 %all-gather.5.cloned.1.call-start = ((), (), s32[]{:S(2)}) async-start(), calls=%async_computation.5 | async-start | bytes 2162688 | tf_op jit(solution)/shard_map/all_gather | solution.py:155
  48.3 329.1 %reduce-scatter.5.cloned.1.call-start = ((), (), s32[]{:S(2)}) async-start(), calls=%async_computation.7 | async-start | bytes 4325376 | tf_op jit(solution)/shard_map/reduce_scatter | solution.py:163
  48.4 29.2 %copy-start.3 = (s32[32,8]{1,0:T(8,128)}, s32[32,8]{1,0:T(8,128)S(1)}, u32[]{:S(2)}) copy-start(s32[32,8]{1,0:T(8,128)S(1)} %dynamic-slice_add_fusion) | copy-start | bytes 3076
  297.0 166.2 %reduce-scatter.3.cloned.1.call-start = ((), (), s32[]{:S(2)}) async-start(), calls=%async_computation.6 | async-start | bytes 4325376 | tf_op jit(solution)/shard_map/reduce_scatter | solution.py:162
Sparse Core Ops, SparseCore 0:
  10.3 53.0 all-gather.2
  65.6 53.5 all-gather.4
  297.1 80.1 reduce-scatter.4
  381.4 81.7 reduce-scatter.2
